TPU v7x, 256 devices: a whole 4x4x8 slice. The times are simulated.
256 devices in a mesh: seq: 32 (over x_hi, z, core), tensor: 8 (over y, x_lo).
Axes of the slice: x: 4 (x_hi: 2, x_lo: 2; x = x_hi * 2 + x_lo), y: 4, z: 8, core: 2. Of those that a mesh axis runs over, the one named last changes fastest.
Arguments:
- tokens: bfloat16 [4, 1024, 4096], P(None, 'seq', 'tensor'), may hold values from -600 to 600
- norm_gain: bfloat16 [4096], replicated, may hold values from 0.099609375 to 1.8984375
- w_query: bfloat16 [4096, 2048], P(None, 'tensor'), may hold values from -0.1875 to 0.1875
- w_key: bfloat16 [4096, 2048], P(None, 'tensor'), may hold values from -0.09375 to 0.09375
- w_value: bfloat16 [4096, 2048], P(None, 'tensor'), may hold values from -0.09375 to 0.09375
- w_out: bfloat16 [2048, 4096], P('tensor'), may hold values from -1 to 1
- cache_keys: bfloat16 [4, 8192, 2048], P(None, 'seq', 'tensor'), may hold values from -103 to 103
- cache_values: bfloat16 [4, 8192, 2048], P(None, 'seq', 'tensor'), may hold values from -6 to 6
- cache_len: int32 [4], replicated, may hold values from 1 to 8192, as said below
- group_len: int32 [4], replicated, may hold values from 1 to 1024, 3584 in all
Outputs:
- mixed: bfloat16 [4, 1024, 4096], P(None, 'seq', 'tensor')
- new_keys: bfloat16 [4, 1024, 2048], P(None, 'seq', 'tensor')
- new_values: bfloat16 [4, 1024, 2048], P(None, 'seq', 'tensor')
Inputs may be any that keep to these rules, and one draw needn't show every extreme that they name: `cache_len`: one request's cache holds all 8192 positions. `group_len`: the new-token counts sum to 3584.
All inputs are finite; a program needn't handle non-finite values.
Results may differ from a plain program's by a relative error of at most 0.0075.
The roundings to bfloat16 on the way count: a program that leaves them out, or rounds other values in their place, can miss the bound.
Values may be sent and summed in bfloat16 or wider, within the bound.
No kernel may reach another device: no remote copies, remote signals or barrier semaphores. Data moves between devices by JAX's collectives and lax.ppermute only.
A program may use at most 128 MiB of HBM per device.

v0:
```python
import jax
import jax.numpy as jnp
from jax import lax
from jax.sharding import PartitionSpec as P

HD = 128


def rotate(vector, position):
    half_dim = vector.shape[-1] // 2
    frequency = 1000000.0 ** (-(jnp.arange(half_dim, dtype=jnp.float32) * 2.0 / vector.shape[-1]))
    angles = position.astype(jnp.float32)[..., None] * frequency
    cosine = jnp.concatenate([jnp.cos(angles), jnp.cos(angles)], -1)[..., None, :]
    sine = jnp.concatenate([jnp.sin(angles), jnp.sin(angles)], -1)[..., None, :]
    turned = jnp.concatenate([-vector[..., half_dim:], vector[..., :half_dim]], -1)
    return vector * cosine + turned * sine


def body(
    tokens,
    norm_gain,
    w_query,
    w_key,
    w_value,
    w_out,
    cache_keys,
    cache_values,
    cache_len,
    group_len,
):
    seq_index = lax.axis_index("seq")
    requests, local_rows, width_part = tokens.shape
    gathered = lax.all_gather(tokens, "tensor", axis=2, tiled=True).astype(jnp.float32)
    inverse_rms = lax.rsqrt(jnp.mean(gathered * gathered, -1, keepdims=True) + 1e-05)
    normed = (gathered * inverse_rms * norm_gain.astype(jnp.float32)).astype(jnp.bfloat16)
    flat_rows = normed.reshape(requests * local_rows, -1)
    heads_width = w_query.shape[1]
    local_heads = heads_width // HD

    def project(weight):
        return jnp.dot(flat_rows, weight, preferred_element_type=jnp.float32).reshape(
            requests, local_rows, local_heads, HD
        )

    offsets = jnp.arange(local_rows, dtype=jnp.int32)
    first_row = seq_index * local_rows
    position = cache_len[:, None] + first_row + offsets[None, :]
    queries = (
        rotate(project(w_query), position)
        .astype(jnp.bfloat16)
        .reshape(requests, local_rows, heads_width)
    )
    key_new = (
        rotate(project(w_key), position)
        .astype(jnp.bfloat16)
        .reshape(requests, local_rows, heads_width)
    )
    value_new = project(w_value).astype(jnp.bfloat16).reshape(requests, local_rows, heads_width)
    live_rows = (first_row + offsets)[None, :] < group_len[:, None]
    new_keys = jnp.where(live_rows[..., None], key_new, jnp.zeros_like(key_new))
    new_values = jnp.where(live_rows[..., None], value_new, jnp.zeros_like(value_new))
    all_queries = lax.all_gather(queries, "seq", axis=1, tiled=True)
    group_total = all_queries.shape[1]
    cache_slots = cache_keys.shape[1]
    block_keys = cache_slots + local_rows
    slot_index = seq_index * cache_slots + jnp.arange(cache_slots, dtype=jnp.int32)
    query_index = jnp.arange(group_total, dtype=jnp.int32)
    token_index = first_row + offsets
    score_scale = HD ** (-0.5)
    numer_list = []
    peak_list = []
    mass_list = []
    for request in range(requests):
        query_rows = all_queries[request].reshape(group_total, local_heads, HD)
        key_rows = jnp.concatenate([cache_keys[request], key_new[request]], 0).reshape(
            block_keys, local_heads, HD
        )
        value_rows = jnp.concatenate([cache_values[request], value_new[request]], 0).reshape(
            block_keys, local_heads, HD
        )
        scores = (
            jnp.einsum("qhd,khd->hqk", query_rows, key_rows, preferred_element_type=jnp.float32)
            * score_scale
        )
        cache_ok = slot_index < cache_len[request]
        group_ok = (token_index[None, :] <= query_index[:, None]) & (
            token_index < group_len[request]
        )[None, :]
        usable = jnp.concatenate(
            [jnp.broadcast_to(cache_ok[None, :], (group_total, cache_slots)), group_ok], 1
        )[None]
        row_peak = jnp.max(jnp.where(usable, scores, -1e30), -1)
        weights = jnp.where(usable, jnp.exp(scores - row_peak[..., None]), 0.0)
        row_mass = jnp.sum(weights, -1)
        numer_list.append(
            jnp.einsum(
                "hqk,khd->qhd",
                weights.astype(jnp.bfloat16),
                value_rows,
                preferred_element_type=jnp.float32,
            )
        )
        peak_list.append(row_peak.T)
        mass_list.append(row_mass.T)
    numerators = jnp.stack(numer_list)
    row_peaks = jnp.stack(peak_list)
    row_masses = jnp.stack(mass_list)
    top_peak = lax.pmax(row_peaks.astype(jnp.bfloat16), "seq").astype(row_peaks.dtype)
    factor = jnp.exp(row_peaks - top_peak)
    scaled = (numerators * factor[..., None]).reshape(requests, group_total, heads_width)
    numer_sum, mass_sum = (
        lax.psum_scatter(scaled, "seq", scatter_dimension=1, tiled=True),
        lax.psum_scatter(row_masses * factor, "seq", scatter_dimension=1, tiled=True),
    )
    attended = numer_sum.reshape(requests, local_rows, local_heads, HD) / mass_sum[..., None]
    attended = (
        jnp.where(live_rows[..., None, None], attended, 0.0)
        .astype(jnp.bfloat16)
        .reshape(requests * local_rows, heads_width)
    )
    partial_out = jnp.dot(attended, w_out, preferred_element_type=jnp.float32).reshape(
        requests, local_rows, -1
    )
    mixed = lax.psum_scatter(partial_out, "tensor", scatter_dimension=2, tiled=True).astype(
        jnp.bfloat16
    )
    return (mixed, new_keys, new_values)


def solution(mesh):
    placed = (
        P(None, "seq", "tensor"),
        P(),
        P(None, "tensor"),
        P(None, "tensor"),
        P(None, "tensor"),
        P("tensor", None),
        P(None, "seq", "tensor"),
        P(None, "seq", "tensor"),
        P(),
        P(),
    )
    return jax.shard_map(
        body,
        mesh=mesh,
        in_specs=placed,
        out_specs=(P(None, "seq", "tensor"), P(None, "seq", "tensor"), P(None, "seq", "tensor")),
        check_vma=False,
    )
```

profile of v0, /device:TPU:1, one launch (start us, length us, event | category | flops | bytes accessed | tf_op | source)
XLA Modules:
  0.0 643.1 jit_solution(6151474447986249479)
XLA Ops:
  8.7 4.1 copy.101
  12.8 4.1 copy.100
  17.4 34.0 %all-gather.3.cloned.1.call-done = bf16[4,32,4096]{2,1,0:T(8,128)(2,1)} async-done(((bf16[4,32,512]{2,1,0:T(8,128)(2,1)}), bf16[4,32,4096]{2,1,0:T(8,128)(2,1)}) %all-gather.3.cloned.1.call-update) | async-done | bytes 1048592 | tf_op jit(solution)/shard_map/all_gather | solution.py:33
  51.4 1.7 fusion
  53.1 2.8 fusion.77
  58.9 4.1 copy.99
  63.7 1.0 copy.105
  66.1 1.2 fusion.84
  67.4 1.0 copy.108
  69.1 1.0 copy.107
  70.9 1.2 fusion.82
  76.3 1.3 broadcast_compare_fusion.1
  77.6 1.4 broadcast_compare_fusion.3
  79.3 0.9 pad_add_fusion.1
  81.8 2.8 convolution_convert_fusion
  85.2 57.2 %all-gather.5.cloned.1.call-done = bf16[4,1024,256]{2,1,0:T(8,128)(2,1)} async-done(((bf16[4,32,256]{2,1,0:T(8,128)(2,1)}), bf16[4,1024,256]{2,1,0:T(8,128)(2,1)}) %all-gather.5.cloned.1.call-update) | async-done | bytes 2097168 | tf_op jit(solution)/shard_map/all_gather | solution.py:62
  142.5 2.8 fusion.104
  145.3 1.2 copy.63
  147.2 1.2 fusion.5
  148.4 1.8 fusion.19
  150.2 1.6 copy.86
  151.7 2.1 copy.70
  153.8 1.8 select_reduce_fusion.2
  155.7 1.2 fusion.7
  156.8 1.8 fusion.17
  158.6 2.5 copy.87
  161.2 2.0 copy.76
  163.2 1.9 select_reduce_fusion.1
  165.1 1.2 fusion.9
  166.3 1.8 fusion.15
  168.1 2.6 copy.88
  170.7 2.0 copy.82
  172.7 3.2 select_reduce_fusion
  176.5 124.7 %pmax.7 = bf16[4,1024,2]{1,2,0:T(2,128)(2,1)S(1)} all-reduce(bf16[4,1024,2]{1,2,0:T(2,128)(2,1)} %fusion.103), channel_id=1, replica_groups=mesh['seq'=32,'tensor'=8] {'seq'}, use_global_device_ids=true, to_apply=%region_5.6 | all-reduce | flops 8192 | bytes 32768 | tf_op jit(solution)/shard_map/pmax | solution.py:108
  301.3 2.3 fusion.11
  304.2 2.7 copy.90
  307.0 7.0 %mul.122 = f32[4,1024,2,128]{3,2,1,0:T(2,128)} broadcast(f32[4,1024,2]{2,1,0:T(8,128)} %copy.90), dimensions={0,1,2} | broadcast | bytes 4227072 | tf_op jit(solution)/shard_map/mul | solution.py:110
  314.0 6.4 mul.123
  320.4 3.6 fusion.13
  324.0 2.5 copy.89
  326.5 2.4 copy.102
  329.0 3.0 reshape.250
  332.1 5.6 maximum_multiply_fusion
  338.5 105.2 %reduce-scatter.10.cloned.1.call-done = f32[32,8]{1,0:T(8,128)} async-done(((f32[1024,8]{1,0:T(8,128)}), f32[32,8]{1,0:T(8,128)}) %reduce-scatter.10.cloned.1.call-update) | async-done | bytes 1040
  444.8 129.3 %reduce-scatter.6.cloned.1.call-done = f32[4,32,256]{2,1,0:T(8,128)} async-done(((f32[4,1024,256]{2,1,0:T(8,128)}), f32[4,32,256]{2,1,0:T(8,128)}) %reduce-scatter.6.cloned.1.call-update) | async-done | bytes 131088 | tf_op jit(solution)/shard_map/reduce_scatter | solution.py:112
  574.1 2.7 fusion.3
  577.6 57.4 %reduce-scatter.8.cloned.1.call-done = f32[4,32,512]{2,1,0:T(8,128)} async-done(((f32[4,32,4096]{2,1,0:T(8,128)}), f32[4,32,512]{2,1,0:T(8,128)}) %reduce-scatter.8.cloned.1.call-update) | async-done | bytes 262160 | tf_op jit(solution)/shard_map/reduce_scatter | solution.py:124
  635.0 1.6 convert_element_type.66
  (108 shorter events, 19.9 us)
Async XLA Ops:
  7.2 567.0 %copy-start = (bf16[256,4096]{1,0:T(8,128)(2,1)S(1)}, bf16[256,4096]{1,0:T(8,128)(2,1)}, u32[]{:S(2)}) copy-start(bf16[256,4096]{1,0:T(8,128)(2,1)} %param.15) | copy-start | bytes 6291460
  7.2 44.2 %all-gather.3.cloned.1.call-start = ((), (), s32[]{:S(2)}) async-start(), calls=%async_computation.3 | async-start | bytes 1179648 | tf_op jit(solution)/shard_map/all_gather | solution.py:33
  7.9 134.6 %all-gather.5.cloned.1.call-start = ((), (), s32[]{:S(2)}) async-start(), calls=%async_computation.4 | async-start | bytes 2162688 | tf_op jit(solution)/shard_map/all_gather | solution.py:62
  12.7 4.2 copy-start.18
  51.4 4.5 copy-start.3
  51.4 4.5 copy-start.4
  53.1 3.7 copy-start.21
  55.9 2.1 copy-start.5
  57.7 386.0 %reduce-scatter.10.cloned.1.call-start = ((), (), s32[]{:S(2)}) async-start(), calls=%async_computation.7 | async-start | bytes 540672
  58.6 4.3 copy-start.6
  63.0 12.7 %copy-start.19 = (s32[4]{0:T(128)S(1)}, s32[4]{0:T(128)}, u32[]{:S(2)}) copy-start(s32[4]{0:T(128)} %param.19) | copy-start | bytes 52
  67.4 14.5 %copy-start.22 = (f32[4,32]{1,0:T(4,128)S(1)}, f32[4,32]{1,0:T(4,128)}, u32[]{:S(2)}) copy-start(f32[4,32]{1,0:T(4,128)} %copy-done.21) | copy-start | bytes 1540
  75.6 9.0 %copy-start.23 = (s32[32]{0:T(128)}, s32[32]{0:T(128)S(1)}, u32[]{:S(2)}) copy-start(s32[32]{0:T(128)S(1)} %iota_add_fusion.1) | copy-start | bytes 388
  84.6 62.0 %copy-start.7 = (bf16[4,32,2,128]{3,1,2,0:T(8,128)(2,1)}, bf16[4,32,2,128]{3,1,2,0:T(8,128)(2,1)S(1)}, u32[]{:S(2)}) copy-start(bf16[4,32,2,128]{3,1,2,0:T(8,128)(2,1)S(1)} %convolution_convert_fusion) | copy-start | bytes 196612
  146.6 1.8 copy-start.9
  153.8 1.9 copy-start.2
  153.8 3.0 copy-start.10
  153.8 3.0 copy-start.17
  163.2 1.9 copy-start.1
  163.2 3.0 copy-start.11
  163.2 3.0 copy-start.16
  301.3 2.3 copy-start.12
  301.3 2.3 copy-start.13
  301.3 2.3 copy-start.14
  314.0 6.4 copy-start.15
  332.0 242.1 %reduce-scatter.6.cloned.1.call-start = ((), (), s32[]{:S(2)}) async-start(), calls=%async_computation.5 | async-start | bytes 4325376 | tf_op jit(solution)/shard_map/reduce_scatter | solution.py:112
  337.7 0.7 copy-start.20
  337.7 0.7 copy-start.24
  337.8 297.2 %reduce-scatter.8.cloned.1.call-start = ((), (), s32[]{:S(2)}) async-start(), calls=%async_computation.6 | async-start | bytes 2359296 | tf_op jit(solution)/shard_map/reduce_scatter | solution.py:124
  444.8 132.0 %copy-start.8 = (bf16[4,32,2,128]{3,1,2,0:T(8,128)(2,1)S(1)}, bf16[4,32,2,128]{3,1,2,0:T(8,128)(2,1)}, u32[]{:S(2)}) copy-start(bf16[4,32,2,128]{3,1,2,0:T(8,128)(2,1)} %copy-done.7) | copy-start | bytes 196612
Sparse Core Ops, SparseCore 0:
  9.8 41.5 all-gather.2
  57.8 84.5 all-gather.4
  332.2 111.4 reduce-scatter.9
  447.8 126.3 reduce-scatter.5
  577.0 57.9 reduce-scatter.7
where the time goes:
time: 645 us; the launch traced here: 643 us
  waiting for transfers between devices  384 us (60%)
  blocking collectives  125 us (19%)
  local copies, waits for them, and re-layouts  68.8 us (11%)
  matrix products  25.7 us (4%)
  other arithmetic  25.6 us (4%)
  between operations  14.2 us (2%)
    reduce_scatter x1, waiting for transfers between devices, body(): lax.psum_scatter(scaled, 'seq', scatter_dimension=1, tiled=True)  129 us
    pmax x1, blocking collectives, body(): lax.pmax(row_peaks.astype(jnp.bfloat16), 'seq').astype(row_peaks.dtype)  125 us
    unnamed x6, waiting for transfers between devices  106 us
    reduce_scatter x1, waiting for transfers between devices, body(): lax.psum_scatter(partial_out, 'tensor', scatter_dimension=2, tiled=True)  57.4 us
    all_gather x1, waiting for transfers between devices, body(): all_queries = lax.all_gather(queries, 'seq', axis=1, tiled=True)  57.2 us
    all_gather x1, waiting for transfers between devices, body(): lax.all_gather(tokens, 'tensor', axis=2, tiled=True).astype(jnp.float32)  34 us
    mul x2, local copies, waits for them, and re-layouts, body(): numerators * factor[..., None]  13.4 us
  transfers between devices with their start and end apart: 5, of which 5 were waited for; matrix products, arithmetic and copies ran while one was open for 7% of the time, Pallas kernels for 0%

commit v1 on v0

--- a/solution.py
+++ b/solution.py
@@ -30,7 +30,19 @@
 ):
     seq_index = lax.axis_index("seq")
     requests, local_rows, width_part = tokens.shape
-    gathered = lax.all_gather(tokens, "tensor", axis=2, tiled=True).astype(jnp.float32)
+
+    def read_group(x_in):
+        return jnp.concatenate(
+            lax.all_to_all(
+                jnp.stack(tuple((x_in for _ in range(lax.axis_size("tensor")))), axis=0),
+                axis_name="tensor",
+                split_axis=0,
+                concat_axis=0,
+            ),
+            axis=2,
+        )
+
+    gathered = read_group(tokens).astype(jnp.float32)
     inverse_rms = lax.rsqrt(jnp.mean(gathered * gathered, -1, keepdims=True) + 1e-05)
     normed = (gathered * inverse_rms * norm_gain.astype(jnp.float32)).astype(jnp.bfloat16)
     flat_rows = normed.reshape(requests * local_rows, -1)

time: 645 us -> 614 us (0.952)
  waiting for transfers between devices: 384 us -> 352 us
    all_gather x1 -> x0, waiting for transfers between devices: 34 us -> none  [body(): lax.all_gather(tokens, 'tensor', axis=2, tiled=True).astype(jnp.float32)]
    unnamed x6 -> x5, waiting for transfers between devices: 106 us -> 105 us
where the time goes in v1:
time: 614 us; the launch traced here: 613 us
  waiting for transfers between devices  352 us (57%)
  blocking collectives  125 us (20%)
  local copies, waits for them, and re-layouts  71.7 us (12%)
  matrix products  22.5 us (4%)
  other arithmetic  22.3 us (4%)
  between operations  14.2 us (2%)
    reduce_scatter x1, waiting for transfers between devices, body(): lax.psum_scatter(scaled, 'seq', scatter_dimension=1, tiled=True)  129 us
    pmax x1, blocking collectives, body(): lax.pmax(row_peaks.astype(jnp.bfloat16), 'seq').astype(row_peaks.dtype)  125 us
    unnamed x5, waiting for transfers between devices  105 us
    reduce_scatter x1, waiting for transfers between devices, body(): lax.psum_scatter(partial_out, 'tensor', scatter_dimension=2, tiled=True)  57.3 us
    all_gather x1, waiting for transfers between devices, body(): all_queries = lax.all_gather(queries, 'seq', axis=1, tiled=True)  54.7 us
    mul x2, local copies, waits for them, and re-layouts, body(): numerators * factor[..., None]  13.4 us
    dot_general x3, local copies, waits for them, and re-layouts, project(): jnp.dot(flat_rows, weight, preferred_element_type=jnp.float32)  12.4 us
  transfers between devices with their start and end apart: 5, of which 5 were waited for; matrix products, arithmetic and copies ran while one was open for 7% of the time, Pallas kernels for 0%

profile of v1, /device:TPU:1, one launch (start us, length us, event | category | flops | bytes accessed | tf_op | source)
XLA Modules:
  0.0 613.2 jit_solution(8695356726368112036)
XLA Ops:
  7.2 2.2 stack.56
  9.3 5.9 all-to-all-start
  15.4 4.1 copy.138
  19.5 4.1 copy.137
  24.1 5.7 all-to-all-done
  31.1 1.3 reshape.301
  32.4 2.9 fusion.38
  38.1 4.1 copy.136
  43.0 1.0 copy.142
  45.4 1.3 fusion.84
  46.8 1.0 copy.145
  50.3 1.2 fusion.82
  55.7 1.3 broadcast_compare_fusion.1
  57.0 1.3 broadcast_compare_fusion.3
  61.1 2.8 convolution_convert_fusion
  64.5 54.7 %all-gather.2.cloned.1.call-done = bf16[4,1024,256]{2,1,0:T(8,128)(2,1)} async-done(((bf16[4,32,256]{2,1,0:T(8,128)(2,1)}), bf16[4,1024,256]{2,1,0:T(8,128)(2,1)}) %all-gather.2.cloned.1.call-update) | async-done | bytes 2097168 | tf_op jit(solution)/shard_map/all_gather | solution.py:74
  119.2 2.8 fusion.104
  122.1 1.2 copy.100
  124.0 1.2 fusion.5
  125.1 1.8 fusion.19
  127.0 1.6 copy.123
  128.5 2.1 copy.107
  130.6 1.8 select_reduce_fusion.2
  132.4 1.1 fusion.7
  133.6 1.8 fusion.17
  135.4 2.6 copy.124
  138.0 2.1 copy.113
  140.1 1.9 select_reduce_fusion.1
  142.0 1.2 fusion.9
  143.1 1.8 fusion.15
  144.9 2.6 copy.125
  147.5 2.1 copy.119
  149.5 1.8 select_reduce_fusion
  151.3 1.2 fusion.11
  152.5 1.8 fusion.13
  154.3 2.7 copy.126
  157.1 124.5 %pmax.7 = bf16[4,1024,2]{1,2,0:T(2,128)(2,1)S(1)} all-reduce(bf16[4,1024,2]{1,2,0:T(2,128)(2,1)S(1)} %fusion.103), channel_id=1, replica_groups=mesh['seq'=32,'tensor'=8] {'seq'}, use_global_device_ids=true, to_apply=%region_5.6 | all-reduce | flops 8192 | bytes 32768 | tf_op jit(solution)/shard_map/pmax | solution.py:120
  282.4 2.0 copy.127
  284.4 7.0 %mul.158 = f32[4,1024,2,128]{3,2,1,0:T(2,128)} broadcast(f32[4,1024,2]{2,1,0:T(8,128)} %copy.127), dimensions={0,1,2} | broadcast | bytes 4227072 | tf_op jit(solution)/shard_map/mul | solution.py:122
  291.4 6.4 %mul.159 = f32[4,1024,256]{2,1,0:T(8,128)} reshape(f32[4,1024,2,128]{3,2,1,0:T(2,128)} %mul.158) | data formatting | bytes 8388608 | tf_op jit(solution)/shard_map/mul | solution.py:122
  297.8 1.7 copy.139
  299.5 3.0 reshape.307
  302.6 5.6 maximum_multiply_fusion
  309.0 104.6 %reduce-scatter.10.cloned.1.call-done = f32[32,8]{1,0:T(8,128)} async-done(((f32[1024,8]{1,0:T(8,128)}), f32[32,8]{1,0:T(8,128)}) %reduce-scatter.10.cloned.1.call-update) | async-done | bytes 1040
  414.8 129.5 %reduce-scatter.6.cloned.1.call-done = f32[4,32,256]{2,1,0:T(8,128)} async-done(((f32[4,1024,256]{2,1,0:T(8,128)}), f32[4,32,256]{2,1,0:T(8,128)}) %reduce-scatter.6.cloned.1.call-update) | async-done | bytes 131088 | tf_op jit(solution)/shard_map/reduce_scatter | solution.py:124
  544.3 2.7 fusion.3
  547.8 57.3 %reduce-scatter.8.cloned.1.call-done = f32[4,32,512]{2,1,0:T(8,128)} async-done(((f32[4,32,4096]{2,1,0:T(8,128)}), f32[4,32,512]{2,1,0:T(8,128)}) %reduce-scatter.8.cloned.1.call-update) | async-done | bytes 262160 | tf_op jit(solution)/shard_map/reduce_scatter | solution.py:136
  605.1 1.6 convert_element_type.98
  (109 shorter events, 20.8 us)
Async XLA Ops:
  7.2 537.1 %copy-start = (bf16[256,4096]{1,0:T(8,128)(2,1)S(1)}, bf16[256,4096]{1,0:T(8,128)(2,1)}, u32[]{:S(2)}) copy-start(bf16[256,4096]{1,0:T(8,128)(2,1)} %param.15) | copy-start | bytes 6291460
  7.2 8.1 %copy-start.18 = (bf16[4096]{0:T(1024)(128)(2,1)S(1)}, bf16[4096]{0:T(1024)(128)(2,1)}, u32[]{:S(2)}) copy-start(bf16[4096]{0:T(1024)(128)(2,1)} %param.11) | copy-start | bytes 24580
  9.3 20.5 %all-to-all-start = ((bf16[8,4,32,512]{3,2,1,0:T(8,128)(2,1)}), bf16[8,4,32,512]{3,2,1,0:T(8,128)(2,1)S(1)}, u32[]{:S(2)}, u32[]{:S(2)}) async-start(bf16[8,4,32,512]{3,2,1,0:T(8,128)(2,1)} %stack.56), calls=%async_computation | async-start | bytes 2097152 | tf_op jit(solution)/shard_map/all_to_all | solution.py:36
  15.3 103.9 %all-gather.2.cloned.1.call-start = ((), (), s32[]{:S(2)}) async-start(), calls=%async_computation.4 | async-start | bytes 2162688 | tf_op jit(solution)/shard_map/all_gather | solution.py:74
  19.5 4.1 copy-start.19
  32.4 2.9 copy-start.3
  32.4 2.9 copy-start.4
  35.3 1.9 copy-start.5
  37.1 376.5 %reduce-scatter.10.cloned.1.call-start = ((), (), s32[]{:S(2)}) async-start(), calls=%async_computation.7 | async-start | bytes 540672
  37.9 4.4 copy-start.6
  42.2 12.8 %copy-start.20 = (s32[4]{0:T(128)S(1)}, s32[4]{0:T(128)}, u32[]{:S(2)}) copy-start(s32[4]{0:T(128)} %param.19) | copy-start | bytes 52
  55.0 8.8 %copy-start.22 = (s32[32]{0:T(128)}, s32[32]{0:T(128)S(1)}, u32[]{:S(2)}) copy-start(s32[32]{0:T(128)S(1)} %iota_add_fusion.1) | copy-start | bytes 388
  63.8 59.5 %copy-start.7 = (bf16[4,32,2,128]{3,1,2,0:T(8,128)(2,1)}, bf16[4,32,2,128]{3,1,2,0:T(8,128)(2,1)S(1)}, u32[]{:S(2)}) copy-start(bf16[4,32,2,128]{3,1,2,0:T(8,128)(2,1)S(1)} %convolution_convert_fusion) | copy-start | bytes 196612
  123.3 1.8 copy-start.9
  130.6 1.9 copy-start.2
  130.6 3.0 copy-start.11
  130.6 3.0 copy-start.17
  140.1 1.9 copy-start.1
  140.1 3.0 copy-start.12
  140.1 3.0 copy-start.16
  149.5 3.0 copy-start.10
  149.5 3.0 copy-start.15
  152.5 129.1 %copy-start.13 = (f32[2,1024]{1,0:T(2,128)S(1)}, f32[2,1024]{1,0:T(2,128)}, u32[]{:S(2)}) copy-start(f32[2,1024]{1,0:T(2,128)} %fusion.5) | copy-start | bytes 24580
  152.5 129.1 %copy-start.14 = (f32[2,1024]{1,0:T(2,128)S(1)}, f32[2,1024]{1,0:T(2,128)}, u32[]{:S(2)}) copy-start(f32[2,1024]{1,0:T(2,128)} %fusion.7) | copy-start | bytes 24580
  302.6 241.7 %reduce-scatter.6.cloned.1.call-start = ((), (), s32[]{:S(2)}) async-start(), calls=%async_computation.5 | async-start | bytes 4325376 | tf_op jit(solution)/shard_map/reduce_scatter | solution.py:124
  308.3 0.7 copy-start.21
  308.3 0.7 copy-start.23
  308.3 296.8 %reduce-scatter.8.cloned.1.call-start = ((), (), s32[]{:S(2)}) async-start(), calls=%async_computation.6 | async-start | bytes 2359296 | tf_op jit(solution)/shard_map/reduce_scatter | solution.py:136
  414.8 132.3 %copy-start.8 = (bf16[4,32,2,128]{3,1,2,0:T(8,128)(2,1)S(1)}, bf16[4,32,2,128]{3,1,2,0:T(8,128)(2,1)}, u32[]{:S(2)}) copy-start(bf16[4,32,2,128]{3,1,2,0:T(8,128)(2,1)} %copy-done.7) | copy-start | bytes 196612
Sparse Core Ops, SparseCore 0:
  37.2 81.9 all-gather.1
  302.7 110.8 reduce-scatter.9
  417.9 126.3 reduce-scatter.5
  547.2 57.8 reduce-scatter.7
